TPU v7x, 256 devices: a whole 4x4x8 slice. The times are simulated.
256 devices in a mesh: feeder: 32 (over z_hi, y, core), factor: 8 (over z_lo, x).
Axes of the slice: x: 4, y: 4, z: 8 (z_hi: 4, z_lo: 2; z = z_hi * 2 + z_lo), core: 2. Of those that a mesh axis runs over, the one named last changes fastest.
Arguments:
- sensitivity: bfloat16 [32, 2048, 2048], P('feeder'), may hold values from -0.015625 to 0.015625
- headroom: float32 [32, 8, 2048], P('feeder'), may hold values from 0 to 3
- ev_power: float32 [32, 8, 256], P('feeder'), may hold values from 0.5 to 4
- ev_node: int32 [32, 8, 256], P('feeder'), may hold values from 0 to 2047
- region_map: int32 [32, 256], P('feeder'), may hold values from 0 to 511
- loadings: float32 [512, 8, 512], P('feeder', None, 'factor'), may hold values from -8 to 8
Outputs:
- margin: float32 [32, 8, 2048], P('feeder')
- new_loadings: float32 [512, 8, 512], P('feeder', None, 'factor')
All inputs are finite; a program needn't handle non-finite values.
Results may differ from a plain program's by a relative error of at most 0.0031.
Values may be sent and summed in bfloat16 or wider, within the bound.
No kernel may reach another device: no remote copies, remote signals or barrier semaphores. Data moves between devices by JAX's collectives and lax.ppermute only.
A program may use at most 64 MiB of HBM per device.

v0:
```python
import jax
import jax.numpy as jnp
from jax import lax
from jax.sharding import PartitionSpec as P

quantile = 1.645
epsilon = 1e-06
step_size = 16.0


def shards(sensitivity, headroom, ev_power, ev_node, region_map, loadings):
    members = sensitivity.shape[0]
    ev_count = ev_power.shape[2]
    reg_local, hours, columns = loadings.shape
    total_regions = reg_local * lax.axis_size("feeder")
    packed = loadings.astype(jnp.bfloat16).reshape(reg_local, hours * columns)
    regions = region_map.reshape(-1)
    shard_rows = lax.all_gather(packed, "feeder", axis=0, tiled=True)
    row_count = shard_rows.shape[0]
    matches = (regions[:, None] == lax.iota(jnp.int32, row_count)[None, :]).astype(jnp.bfloat16)
    looked = jnp.dot(matches, shard_rows, preferred_element_type=jnp.float32)
    volts_list = []
    rows_list = []
    partial_list = []
    member = 0
    for interval in range(hours):
        block = looked[
            member * ev_count : (member + 1) * ev_count,
            interval * columns : (interval + 1) * columns,
        ]
        weighted = (ev_power[member, interval][:, None] * block).astype(jnp.bfloat16)
        sens_rows = jnp.take(sensitivity[member], ev_node[member, interval], axis=0)
        factor_volts = jnp.dot(weighted.T, sens_rows, preferred_element_type=jnp.float32)
        volts_list.append(factor_volts)
        rows_list.append(sens_rows)
        partial_sum = jnp.sum(factor_volts * factor_volts, axis=0)
        partial_list.append(partial_sum)
    variance = jnp.stack(partial_list, axis=0).reshape(members, hours, -1)
    variance = lax.psum(variance, "factor")
    deviation = jnp.sqrt(variance + epsilon)
    margin = headroom - quantile * deviation
    violation = jnp.maximum(-margin, 0.0)
    var_grad = quantile * violation / deviation
    member = 0
    interval_grads = []
    for interval in range(hours):
        position = member * hours + interval
        volt_grad = (2.0 * var_grad[member, interval][None, :] * volts_list[position]).astype(
            jnp.bfloat16
        )
        weight_grad = jnp.dot(rows_list[position], volt_grad.T, preferred_element_type=jnp.float32)
        interval_grads.append(ev_power[member, interval][:, None] * weight_grad)
    member_grads = jnp.concatenate(interval_grads, axis=1)
    offset = regions - 0
    inside = jnp.logical_and(offset >= 0, offset < total_regions)
    target = jnp.where(inside, offset, total_regions)
    summed = jax.ops.segment_sum(member_grads, target, num_segments=total_regions + 1)
    whole_term = summed[:total_regions]
    reduced = lax.psum_scatter(whole_term, "feeder", scatter_dimension=0, tiled=True)
    new_loadings = loadings - step_size * reduced.reshape(reg_local, hours, columns)
    return (margin, new_loadings)


def solution(mesh):
    return jax.shard_map(
        shards,
        mesh=mesh,
        in_specs=(
            P("feeder", None, None),
            P("feeder", None, None),
            P("feeder", None, None),
            P("feeder", None, None),
            P("feeder", None),
            P("feeder", None, "factor"),
        ),
        out_specs=(P("feeder", None, None), P("feeder", None, "factor")),
        check_vma=False,
    )
```

profile of v0, /device:TPU:2, one launch (start us, length us, event | category | flops | bytes accessed | tf_op | source)
XLA Modules:
  0.0 324.0 jit_solution(15895754559689770932)
XLA Ops:
  7.2 0.0 all-reduce.2.cloned.1.call-start
  7.2 1.0 fusion.61
  8.4 1.0 fusion.60
  9.4 0.8 convert_element_type.52
  10.3 0.1 reshape.133
  10.4 49.2 %all_gather.3 = bf16[512,512]{1,0:T(8,128)(2,1)S(1)} all-gather(bf16[16,512]{1,0:T(8,128)(2,1)S(1)} %reshape.133), channel_id=1, replica_groups=mesh['feeder'=32,'factor'=8] {'feeder'}, dimensions={0}, use_global_device_ids=true | all-gather | bytes 540672 | tf_op jit(solution)/shard_map/all_gather | solution.py:18
  59.6 6.8 %gather_fusion.2 = bf16[256,2048]{1,0:T(8,128)(2,1)S(1)} fusion(bf16[2048,2048]{1,0:T(8,128)(2,1)} %bitcast.39, s32[1024]{0:T(1024)S(1)} %pad_clamp_fusion.5), kind=kCustom, calls=%fused_computation.2.clone | custom fusion | bytes 2098176 | tf_op jit(solution)/shard_map/jit(_take)/gather | solution.py:32
  66.4 6.8 %gather_fusion.3 = bf16[256,2048]{1,0:T(8,128)(2,1)S(1)} fusion(bf16[2048,2048]{1,0:T(8,128)(2,1)} %bitcast.40, s32[1024]{0:T(1024)S(1)} %pad_clamp_fusion.4), kind=kCustom, calls=%fused_computation.3.clone | custom fusion | bytes 2098176 | tf_op jit(solution)/shard_map/jit(_take)/gather | solution.py:32
  73.3 7.8 %gather_fusion.4 = bf16[256,2048]{1,0:T(8,128)(2,1)} fusion(bf16[2048,2048]{1,0:T(8,128)(2,1)} %bitcast.41, s32[1024]{0:T(1024)S(1)} %pad_clamp_fusion.3), kind=kCustom, calls=%fused_computation.4.clone | custom fusion | bytes 2098176 | tf_op jit(solution)/shard_map/jit(_take)/gather | solution.py:32
  81.1 8.0 %gather_fusion.5 = bf16[256,2048]{1,0:T(8,128)(2,1)} fusion(bf16[2048,2048]{1,0:T(8,128)(2,1)} %bitcast.42, s32[1024]{0:T(1024)S(1)} %pad_clamp_fusion.2), kind=kCustom, calls=%fused_computation.5.clone | custom fusion | bytes 2098176 | tf_op jit(solution)/shard_map/jit(_take)/gather | solution.py:32
  89.1 7.8 %gather_fusion.6 = bf16[256,2048]{1,0:T(8,128)(2,1)} fusion(bf16[2048,2048]{1,0:T(8,128)(2,1)} %bitcast.43, s32[1024]{0:T(1024)S(1)} %pad_clamp_fusion.1), kind=kCustom, calls=%fused_computation.6.clone | custom fusion | bytes 2098176 | tf_op jit(solution)/shard_map/jit(_take)/gather | solution.py:32
  96.9 7.8 %gather_fusion.7 = bf16[256,2048]{1,0:T(8,128)(2,1)} fusion(bf16[2048,2048]{1,0:T(8,128)(2,1)} %bitcast.44, s32[1024]{0:T(1024)S(1)} %pad_clamp_fusion), kind=kCustom, calls=%fused_computation.7.clone | custom fusion | bytes 2098176 | tf_op jit(solution)/shard_map/jit(_take)/gather | solution.py:32
  104.7 7.9 %gather_fusion.1 = bf16[256,2048]{1,0:T(8,128)(2,1)} fusion(bf16[2048,2048]{1,0:T(8,128)(2,1)} %bitcast.45, s32[1024]{0:T(1024)S(1)} %pad_clamp_fusion.6), kind=kCustom, calls=%fused_computation.1.clone | custom fusion | bytes 2098176 | tf_op jit(solution)/shard_map/jit(_take)/gather | solution.py:32
  112.6 8.0 %gather_fusion = bf16[256,2048]{1,0:T(8,128)(2,1)} fusion(bf16[2048,2048]{1,0:T(8,128)(2,1)} %bitcast.46, s32[1024]{0:T(1024)S(1)} %pad_clamp_fusion.7), kind=kCustom, calls=%fused_computation.clone | custom fusion | bytes 2098176 | tf_op jit(solution)/shard_map/jit(_take)/gather | solution.py:32
  120.6 0.0 copy-done.7
  120.7 0.3 fusion.2
  121.0 1.2 multiply_reduce_fusion.5
  122.2 1.2 multiply_reduce_fusion.4
  123.5 2.5 multiply_reduce_fusion.3
  126.0 2.6 multiply_reduce_fusion.2
  128.5 2.4 multiply_reduce_fusion.1
  131.0 0.0 copy-done.4
  131.0 1.3 multiply_reduce_fusion
  132.2 0.0 copy-done.2
  132.2 1.3 multiply_reduce_fusion.6
  133.5 1.2 multiply_reduce_fusion.7
  134.8 0.7 stack.35
  135.5 0.0 all-reduce.2.cloned.1.call-update
  135.5 0.0 reduce-scatter.2.cloned.1.call-start
  135.6 71.0 %all-reduce.2.cloned.1.call-done = f32[1,8,2048]{2,1,0:T(8,128)} async-done(((f32[1,8,2048]{2,1,0:T(8,128)}), f32[1,8,2048]{2,1,0:T(8,128)}) %all-reduce.2.cloned.1.call-update) | async-done | bytes 65552 | tf_op jit(solution)/shard_map/psum | solution.py:39
  206.6 1.6 multiply_divide_fusion
  208.2 0.1 slice_multiply_fusion.8
  208.3 2.0 convolution_multiply_fusion
  210.2 1.8 convolution_multiply_fusion.1
  212.1 2.5 convolution_multiply_fusion.2
  214.5 2.5 convolution_multiply_fusion.3
  217.1 1.1 convolution_multiply_fusion.4
  218.2 0.5 convolution_multiply_fusion.5
  218.7 0.5 convolution_multiply_fusion.6
  219.3 0.5 convolution_multiply_fusion.7
  219.8 1.3 concatenate.3
  221.1 2.3 scatter_custom_fusion
  223.4 1.1 slice.172
  224.5 0.0 reduce-scatter.2.cloned.1.call-update
  224.5 91.1 %reduce-scatter.2.cloned.1.call-done = f32[16,512]{1,0:T(8,128)} async-done(((f32[512,512]{1,0:T(8,128)}), f32[16,512]{1,0:T(8,128)}) %reduce-scatter.2.cloned.1.call-update) | async-done | bytes 32784 | tf_op jit(solution)/shard_map/reduce_scatter | solution.py:59
  315.6 0.8 broadcast_multiply_fusion
  316.4 0.1 mul.395
  316.5 0.6 sub.7
  (46 shorter events, 0.2 us)
Async XLA Ops:
  7.2 199.4 %all-reduce.2.cloned.1.call-start = ((), (), s32[]{:S(2)}) async-start(), calls=%async_computation.1 | async-start | bytes 131072 | tf_op jit(solution)/shard_map/psum | solution.py:39
  104.7 15.9 %copy-start.7 = (s32[1,256]{1,0:T(1,128)S(1)}, s32[1,256]{1,0:T(1,128)}, u32[]{:S(2)}) copy-start(s32[1,256]{1,0:T(1,128)} %param.12) | copy-start | bytes 3076
  120.6 10.4 %copy-start.4 = (bf16[256,2048]{1,0:T(8,128)(2,1)S(1)}, bf16[256,2048]{1,0:T(8,128)(2,1)}, u32[]{:S(2)}) copy-start(bf16[256,2048]{1,0:T(8,128)(2,1)} %gather_fusion.7) | copy-start | bytes 3145732
  120.6 11.6 %copy-start.2 = (bf16[256,2048]{1,0:T(8,128)(2,1)S(1)}, bf16[256,2048]{1,0:T(8,128)(2,1)}, u32[]{:S(2)}) copy-start(bf16[256,2048]{1,0:T(8,128)(2,1)} %gather_fusion.1) | copy-start | bytes 3145732
  120.6 12.9 %copy-start = (bf16[256,2048]{1,0:T(8,128)(2,1)S(1)}, bf16[256,2048]{1,0:T(8,128)(2,1)}, u32[]{:S(2)}) copy-start(bf16[256,2048]{1,0:T(8,128)(2,1)} %gather_fusion) | copy-start | bytes 3145732
  120.6 85.9 %copy-start.6 = (f32[1,8,2048]{2,1,0:T(8,128)S(1)}, f32[1,8,2048]{2,1,0:T(8,128)}, u32[]{:S(2)}) copy-start(f32[1,8,2048]{2,1,0:T(8,128)} %param.9) | copy-start | bytes 196612
  133.5 85.2 %copy-start.3 = (bf16[256,2048]{1,0:T(8,128)(2,1)S(1)}, bf16[256,2048]{1,0:T(8,128)(2,1)}, u32[]{:S(2)}) copy-start(bf16[256,2048]{1,0:T(8,128)(2,1)} %gather_fusion.1) | copy-start | bytes 3145732
  135.5 180.1 %reduce-scatter.2.cloned.1.call-start = ((), (), s32[]{:S(2)}) async-start(), calls=%async_computation.2 | async-start | bytes 1081344 | tf_op jit(solution)/shard_map/reduce_scatter | solution.py:59
  206.5 10.5 %copy-start.10 = (f32[64,2048]{1,0:T(8,128)S(1)}, f32[64,2048]{1,0:T(8,128)}, u32[]{:S(2)}) copy-start(f32[64,2048]{1,0:T(8,128)} %get-tuple-element.36) | copy-start | bytes 1572868
  206.5 11.7 %copy-start.8 = (f32[64,2048]{1,0:T(8,128)S(1)}, f32[64,2048]{1,0:T(8,128)}, u32[]{:S(2)}) copy-start(f32[64,2048]{1,0:T(8,128)} %get-tuple-element.34) | copy-start | bytes 1572868
  206.5 12.2 %copy-start.11 = (f32[64,2048]{1,0:T(8,128)S(1)}, f32[64,2048]{1,0:T(8,128)}, u32[]{:S(2)}) copy-start(f32[64,2048]{1,0:T(8,128)} %get-tuple-element.32) | copy-start | bytes 1572868
  208.2 11.0 %copy-start.1 = (bf16[256,2048]{1,0:T(8,128)(2,1)S(1)}, bf16[256,2048]{1,0:T(8,128)(2,1)}, u32[]{:S(2)}) copy-start(bf16[256,2048]{1,0:T(8,128)(2,1)} %gather_fusion) | copy-start | bytes 3145732
  208.2 11.0 %copy-start.9 = (f32[64,2048]{1,0:T(8,128)S(1)}, f32[64,2048]{1,0:T(8,128)}, u32[]{:S(2)}) copy-start(f32[64,2048]{1,0:T(8,128)} %get-tuple-element.30) | copy-start | bytes 1572868
  214.5 101.9 %copy-start.5 = (f32[16,8,64]{2,1,0:T(8,128)S(1)}, f32[16,8,64]{2,1,0:T(8,128)}, u32[]{:S(2)}) copy-start(f32[16,8,64]{2,1,0:T(8,128)} %param.13) | copy-start | bytes 98308
Sparse Core Ops, SparseCore 0:
  135.6 70.8 all-reduce.1
  224.6 90.9 reduce-scatter.1
where the time goes:
time: 325 us; the launch traced here: 324 us
  waiting for transfers between devices  162 us (50%)
  local copies, waits for them, and re-layouts  66.3 us (20%)
  blocking collectives  49.2 us (15%)
  matrix products  25.5 us (8%)
  between operations  14.3 us (4%)
  other arithmetic  6.4 us (2%)
    reduce_scatter x1, waiting for transfers between devices, shards(): lax.psum_scatter(whole_term, 'feeder', scatter_dimension=0, tiled=True)  91.1 us
    psum x1, waiting for transfers between devices, shards(): variance = lax.psum(variance, 'factor')  71 us
    gather x8, local copies, waits for them, and re-layouts, shards(): sens_rows = jnp.take(sensitivity[member], ev_node[member, interval], axis=0)  61 us
    all_gather x1, blocking collectives, shards(): shard_rows = lax.all_gather(packed, 'feeder', axis=0, tiled=True)  49.2 us
    dot_general x8, matrix products, shards(): jnp.dot(weighted.T, sens_rows, preferred_element_type=jnp.float32)  13.7 us
    dot_general x8, matrix products, shards(): jnp.dot(rows_list[position], volt_grad.T, preferred_element_type=jnp.floa...  11.4 us
  transfers between devices with their start and end apart: 2, of which 2 were waited for; matrix products, arithmetic and copies ran while one was open for 0% of the time, Pallas kernels for 0%

commit v1 on v0

--- a/solution.py
+++ b/solution.py
@@ -15,7 +15,9 @@
     total_regions = reg_local * lax.axis_size("feeder")
     packed = loadings.astype(jnp.bfloat16).reshape(reg_local, hours * columns)
     regions = region_map.reshape(-1)
-    shard_rows = lax.all_gather(packed, "feeder", axis=0, tiled=True)
+    shard_rows = jnp.concatenate(
+        lax.all_to_all(jnp.stack([packed] * lax.axis_size("feeder")), "feeder", 0, 0), axis=0
+    )
     row_count = shard_rows.shape[0]
     matches = (regions[:, None] == lax.iota(jnp.int32, row_count)[None, :]).astype(jnp.bfloat16)
     looked = jnp.dot(matches, shard_rows, preferred_element_type=jnp.float32)

time: 325 us -> 294 us (0.905)
  blocking collectives: 49.2 us -> 0 us
  starting transfers between devices: 0.08 us -> 11.6 us
  waiting for transfers between devices: 162 us -> 169 us
    all_gather x1 -> x0, blocking collectives: 49.2 us -> none  [shards(): shard_rows = lax.all_gather(packed, 'feeder', axis=0, tiled=True)]
    all_to_all x0 -> x1, starting transfers between devices: none -> 11.5 us  [shards(): lax.all_to_all(jnp.stack([packed] * lax.axis_size('feeder')), 'feeder', 0...]
    psum x1, waiting for transfers between devices: 71 us -> 78.2 us  [shards(): variance = lax.psum(variance, 'factor')]
  transfers between devices with their start and end apart: 2 -> 3, of which waited for: 2 -> 2; matrix products, arithmetic and copies ran while one was open for 0% -> 21% of each run, Pallas kernels for 0% -> 0%
where the time goes in v1:
time: 294 us
  waiting for transfers between devices  169 us (57%)
  local copies, waits for them, and re-layouts  66.2 us (23%)
  matrix products  25.5 us (9%)
  between operations  14.4 us (5%)
  starting transfers between devices  11.6 us (4%)
  other arithmetic  6.41 us (2%)
    reduce_scatter x1, waiting for transfers between devices, shards(): lax.psum_scatter(whole_term, 'feeder', scatter_dimension=0, tiled=True)  91.1 us
    psum x1, waiting for transfers between devices, shards(): variance = lax.psum(variance, 'factor')  78.2 us
    gather x8, local copies, waits for them, and re-layouts, shards(): sens_rows = jnp.take(sensitivity[member], ev_node[member, interval], axis=0)  61 us
    dot_general x8, matrix products, shards(): jnp.dot(weighted.T, sens_rows, preferred_element_type=jnp.float32)  13.7 us
    all_to_all x1, starting transfers between devices, shards(): lax.all_to_all(jnp.stack([packed] * lax.axis_size('feeder')), 'feeder', 0...  11.5 us
    dot_general x8, matrix products, shards(): jnp.dot(rows_list[position], volt_grad.T, preferred_element_type=jnp.floa...  11.4 us
  transfers between devices with their start and end apart: 3, of which 2 were waited for; matrix products, arithmetic and copies ran while one was open for 21% of the time, Pallas kernels for 0%

profile of v1, /device:TPU:2, one launch (start us, length us, event | category | flops | bytes accessed | tf_op | source)
XLA Modules:
  0.0 293.5 jit_solution(11891305600232531640)
XLA Ops:
  7.2 0.8 convert_element_type.52
  8.0 0.1 stack_reshape.2
  8.1 0.9 stack.30
  9.0 11.5 %all-to-all-start = ((bf16[32,16,512]{2,1,0:T(8,128)(2,1)}), bf16[32,16,512]{2,1,0:T(8,128)(2,1)S(1)}, u32[]{:S(2)}, u32[]{:S(2)}) async-start(bf16[32,16,512]{2,1,0:T(8,128)(2,1)} %stack.30), calls=%async_computation | async-start | bytes 1048576 | tf_op jit(solution)/shard_map/all_to_all | solution.py:19
  20.5 0.0 all-reduce.2.cloned.1.call-start
  20.5 1.0 fusion.61
  21.7 6.8 %gather_fusion.2 = bf16[256,2048]{1,0:T(8,128)(2,1)S(1)} fusion(bf16[2048,2048]{1,0:T(8,128)(2,1)} %bitcast.40, s32[1024]{0:T(1024)S(1)} %pad_clamp_fusion.5), kind=kCustom, calls=%fused_computation.2.clone | custom fusion | bytes 2098176 | tf_op jit(solution)/shard_map/jit(_take)/gather | solution.py:34
  28.5 6.8 %gather_fusion.3 = bf16[256,2048]{1,0:T(8,128)(2,1)S(1)} fusion(bf16[2048,2048]{1,0:T(8,128)(2,1)} %bitcast.41, s32[1024]{0:T(1024)S(1)} %pad_clamp_fusion.4), kind=kCustom, calls=%fused_computation.3.clone | custom fusion | bytes 2098176 | tf_op jit(solution)/shard_map/jit(_take)/gather | solution.py:34
  35.3 7.8 %gather_fusion.4 = bf16[256,2048]{1,0:T(8,128)(2,1)} fusion(bf16[2048,2048]{1,0:T(8,128)(2,1)} %bitcast.42, s32[1024]{0:T(1024)S(1)} %pad_clamp_fusion.3), kind=kCustom, calls=%fused_computation.4.clone | custom fusion | bytes 2098176 | tf_op jit(solution)/shard_map/jit(_take)/gather | solution.py:34
  43.2 8.0 %gather_fusion.5 = bf16[256,2048]{1,0:T(8,128)(2,1)} fusion(bf16[2048,2048]{1,0:T(8,128)(2,1)} %bitcast.43, s32[1024]{0:T(1024)S(1)} %pad_clamp_fusion.2), kind=kCustom, calls=%fused_computation.5.clone | custom fusion | bytes 2098176 | tf_op jit(solution)/shard_map/jit(_take)/gather | solution.py:34
  51.2 7.8 %gather_fusion.6 = bf16[256,2048]{1,0:T(8,128)(2,1)} fusion(bf16[2048,2048]{1,0:T(8,128)(2,1)} %bitcast.44, s32[1024]{0:T(1024)S(1)} %pad_clamp_fusion.1), kind=kCustom, calls=%fused_computation.6.clone | custom fusion | bytes 2098176 | tf_op jit(solution)/shard_map/jit(_take)/gather | solution.py:34
  59.0 7.8 %gather_fusion.7 = bf16[256,2048]{1,0:T(8,128)(2,1)} fusion(bf16[2048,2048]{1,0:T(8,128)(2,1)} %bitcast.45, s32[1024]{0:T(1024)S(1)} %pad_clamp_fusion), kind=kCustom, calls=%fused_computation.7.clone | custom fusion | bytes 2098176 | tf_op jit(solution)/shard_map/jit(_take)/gather | solution.py:34
  66.8 0.0 copy-start.7
  66.8 0.0 copy-start.8
  66.8 7.9 %gather_fusion.1 = bf16[256,2048]{1,0:T(8,128)(2,1)} fusion(bf16[2048,2048]{1,0:T(8,128)(2,1)} %bitcast.46, s32[1024]{0:T(1024)S(1)} %pad_clamp_fusion.6), kind=kCustom, calls=%fused_computation.1.clone | custom fusion | bytes 2098176 | tf_op jit(solution)/shard_map/jit(_take)/gather | solution.py:34
  74.7 8.0 %gather_fusion = bf16[256,2048]{1,0:T(8,128)(2,1)} fusion(bf16[2048,2048]{1,0:T(8,128)(2,1)} %bitcast.47, s32[1024]{0:T(1024)S(1)} %pad_clamp_fusion.7), kind=kCustom, calls=%fused_computation.clone | custom fusion | bytes 2098176 | tf_op jit(solution)/shard_map/jit(_take)/gather | solution.py:34
  82.8 0.0 all-to-all-done
  82.9 0.3 fusion.2
  83.2 1.2 multiply_reduce_fusion.5
  84.5 1.2 multiply_reduce_fusion.4
  85.7 2.5 multiply_reduce_fusion.3
  88.2 2.6 multiply_reduce_fusion.2
  90.7 2.5 multiply_reduce_fusion.1
  93.2 1.2 multiply_reduce_fusion
  94.4 1.3 multiply_reduce_fusion.6
  95.7 1.2 multiply_reduce_fusion.7
  97.0 0.7 stack.39
  97.7 0.0 all-reduce.2.cloned.1.call-update
  97.7 0.0 reduce-scatter.2.cloned.1.call-start
  97.8 78.2 %all-reduce.2.cloned.1.call-done = f32[1,8,2048]{2,1,0:T(8,128)} async-done(((f32[1,8,2048]{2,1,0:T(8,128)}), f32[1,8,2048]{2,1,0:T(8,128)}) %all-reduce.2.cloned.1.call-update) | async-done | bytes 65552 | tf_op jit(solution)/shard_map/psum | solution.py:41
  176.1 1.6 multiply_divide_fusion
  177.7 0.1 slice_multiply_fusion.8
  177.8 2.0 convolution_multiply_fusion
  179.7 1.8 convolution_multiply_fusion.1
  181.6 2.5 convolution_multiply_fusion.2
  184.1 2.5 convolution_multiply_fusion.3
  186.6 1.2 convolution_multiply_fusion.4
  187.7 0.5 convolution_multiply_fusion.5
  188.3 0.5 convolution_multiply_fusion.6
  188.8 0.5 convolution_multiply_fusion.7
  189.3 1.3 concatenate.3
  190.6 2.3 scatter_custom_fusion
  193.0 1.1 slice.172
  194.0 0.0 reduce-scatter.2.cloned.1.call-update
  194.0 91.1 %reduce-scatter.2.cloned.1.call-done = f32[16,512]{1,0:T(8,128)} async-done(((f32[512,512]{1,0:T(8,128)}), f32[16,512]{1,0:T(8,128)}) %reduce-scatter.2.cloned.1.call-update) | async-done | bytes 32784 | tf_op jit(solution)/shard_map/reduce_scatter | solution.py:61
  285.2 0.8 broadcast_multiply_fusion
  285.9 0.1 mul.395
  286.0 0.6 sub.7
  (50 shorter events, 0.2 us)
Async XLA Ops:
  9.0 73.8 %all-to-all-start = ((bf16[32,16,512]{2,1,0:T(8,128)(2,1)}), bf16[32,16,512]{2,1,0:T(8,128)(2,1)S(1)}, u32[]{:S(2)}, u32[]{:S(2)}) async-start(bf16[32,16,512]{2,1,0:T(8,128)(2,1)} %stack.30), calls=%async_computation | async-start | bytes 1048576 | tf_op jit(solution)/shard_map/all_to_all | solution.py:19
  20.5 155.6 %all-reduce.2.cloned.1.call-start = ((), (), s32[]{:S(2)}) async-start(), calls=%async_computation.2 | async-start | bytes 131072 | tf_op jit(solution)/shard_map/psum | solution.py:41
  66.8 16.0 %copy-start.7 = (f32[1,8,256]{2,1,0:T(8,128)S(1)}, f32[1,8,256]{2,1,0:T(8,128)}, u32[]{:S(2)}) copy-start(f32[1,8,256]{2,1,0:T(8,128)} %param.10) | copy-start | bytes 24580
  66.8 16.0 %copy-start.8 = (s32[1,256]{1,0:T(1,128)S(1)}, s32[1,256]{1,0:T(1,128)}, u32[]{:S(2)}) copy-start(s32[1,256]{1,0:T(1,128)} %param.12) | copy-start | bytes 3076
  82.7 93.3 %copy-start.6 = (f32[1,8,2048]{2,1,0:T(8,128)S(1)}, f32[1,8,2048]{2,1,0:T(8,128)}, u32[]{:S(2)}) copy-start(f32[1,8,2048]{2,1,0:T(8,128)} %param.9) | copy-start | bytes 196612
  82.8 10.4 %copy-start.4 = (bf16[256,2048]{1,0:T(8,128)(2,1)S(1)}, bf16[256,2048]{1,0:T(8,128)(2,1)}, u32[]{:S(2)}) copy-start(bf16[256,2048]{1,0:T(8,128)(2,1)} %gather_fusion.7) | copy-start | bytes 3145732
  82.8 11.6 %copy-start.2 = (bf16[256,2048]{1,0:T(8,128)(2,1)S(1)}, bf16[256,2048]{1,0:T(8,128)(2,1)}, u32[]{:S(2)}) copy-start(bf16[256,2048]{1,0:T(8,128)(2,1)} %gather_fusion.1) | copy-start | bytes 3145732
  82.9 12.9 %copy-start = (bf16[256,2048]{1,0:T(8,128)(2,1)S(1)}, bf16[256,2048]{1,0:T(8,128)(2,1)}, u32[]{:S(2)}) copy-start(bf16[256,2048]{1,0:T(8,128)(2,1)} %gather_fusion) | copy-start | bytes 3145732
  95.7 92.5 %copy-start.3 = (bf16[256,2048]{1,0:T(8,128)(2,1)S(1)}, bf16[256,2048]{1,0:T(8,128)(2,1)}, u32[]{:S(2)}) copy-start(bf16[256,2048]{1,0:T(8,128)(2,1)} %gather_fusion.1) | copy-start | bytes 3145732
  97.7 187.4 %reduce-scatter.2.cloned.1.call-start = ((), (), s32[]{:S(2)}) async-start(), calls=%async_computation.3 | async-start | bytes 1081344 | tf_op jit(solution)/shard_map/reduce_scatter | solution.py:61
  176.0 10.5 %copy-start.11 = (f32[64,2048]{1,0:T(8,128)S(1)}, f32[64,2048]{1,0:T(8,128)}, u32[]{:S(2)}) copy-start(f32[64,2048]{1,0:T(8,128)} %get-tuple-element.36) | copy-start | bytes 1572868
  176.0 11.7 %copy-start.9 = (f32[64,2048]{1,0:T(8,128)S(1)}, f32[64,2048]{1,0:T(8,128)}, u32[]{:S(2)}) copy-start(f32[64,2048]{1,0:T(8,128)} %get-tuple-element.34) | copy-start | bytes 1572868
  176.0 12.2 %copy-start.12 = (f32[64,2048]{1,0:T(8,128)S(1)}, f32[64,2048]{1,0:T(8,128)}, u32[]{:S(2)}) copy-start(f32[64,2048]{1,0:T(8,128)} %get-tuple-element.32) | copy-start | bytes 1572868
  177.7 11.0 %copy-start.1 = (bf16[256,2048]{1,0:T(8,128)(2,1)S(1)}, bf16[256,2048]{1,0:T(8,128)(2,1)}, u32[]{:S(2)}) copy-start(bf16[256,2048]{1,0:T(8,128)(2,1)} %gather_fusion) | copy-start | bytes 3145732
  177.7 11.0 %copy-start.10 = (f32[64,2048]{1,0:T(8,128)S(1)}, f32[64,2048]{1,0:T(8,128)}, u32[]{:S(2)}) copy-start(f32[64,2048]{1,0:T(8,128)} %get-tuple-element.30) | copy-start | bytes 1572868
  184.1 102.0 %copy-start.5 = (f32[16,8,64]{2,1,0:T(8,128)S(1)}, f32[16,8,64]{2,1,0:T(8,128)}, u32[]{:S(2)}) copy-start(f32[16,8,64]{2,1,0:T(8,128)} %param.13) | copy-start | bytes 98308
Sparse Core Ops, SparseCore 0:
  97.9 78.1 all-reduce.1
  194.2 90.9 reduce-scatter.1
